TPU v7x, 256 devices: a whole 4x4x8 slice. The times are simulated.
256 devices in a mesh: seq: 16 (over x, y), tp: 16 (over z, core).
Axes of the slice: x: 4, y: 4, z: 8, core: 2. Of those that a mesh axis runs over, the one named last changes fastest.
Arguments:
- query: bfloat16 [16384, 8192], P('seq', 'tp'), may hold values from -6 to 6
- key_in: bfloat16 [16384, 8192], P('seq', 'tp'), may hold values from -6 to 6
- value: bfloat16 [16384, 8192], P('seq', 'tp'), may hold values from -6 to 6
- gate: bfloat16 [16384, 8192], P('seq', 'tp'), may hold values from -8 to 8
- kv_start: float32 [64, 128, 128], P('tp'), may hold values from -240 to 240
- norm_gain: float32 [8192], P('tp'), may hold values from 0.5 to 2
- w_out: bfloat16 [8192, 6144], P('tp'), may hold values from -0.0625 to 0.0625
Outputs:
- mixed: bfloat16 [16384, 6144], P(('seq', 'tp'))
All inputs are finite; a program needn't handle non-finite values.
Results may differ from a plain program's by a relative error of at most 0.019.
Values may be sent and summed in bfloat16 or wider, within the bound.
No kernel may reach another device: no remote copies, remote signals or barrier semaphores. Data moves between devices by JAX's collectives and lax.ppermute only.
A program may use at most 128 MiB of HBM per device.

v0:
```python
import jax
import jax.numpy as jnp
from jax import lax
from jax.sharding import PartitionSpec as P

HD = 128


def per_device(query, key_in, value, gate, kv_start, norm_gain, w_out):
    rows = query.shape[0]
    heads = query.shape[1] // HD
    block = min(512, rows)
    count = rows // block
    highest = lax.Precision.HIGHEST
    qa = (
        jax.nn.silu(query.astype(jnp.float32)).astype(jnp.bfloat16).reshape(count, block, heads, HD)
    )
    ka = (
        jax.nn.silu(key_in.astype(jnp.float32))
        .astype(jnp.bfloat16)
        .reshape(count, block, heads, HD)
    )
    va = value.reshape(count, block, heads, HD)
    block_states = jnp.einsum("nthd,nthe->nhde", ka, va, preferred_element_type=jnp.float32)
    own_total = jnp.sum(block_states, axis=0)
    local_before = jnp.cumsum(block_states, axis=0) - block_states
    gathered = lax.all_gather(
        own_total[None].astype(jnp.bfloat16), "seq", axis=0, tiled=True
    ).astype(jnp.float32)
    position = lax.axis_index("seq")
    below = (jnp.arange(gathered.shape[0]) < position).astype(jnp.float32)
    prior = jnp.sum(gathered * below[:, None, None, None], axis=0)
    states = local_before + (kv_start + prior)[None]
    q_float = qa.astype(jnp.float32)
    inter = jnp.einsum("nthd,nhde->nthe", q_float, states, precision=highest)
    scores = jnp.einsum("nthd,nshd->nhts", qa, ka, preferred_element_type=jnp.float32)
    causal = jnp.arange(block)[:, None] >= jnp.arange(block)[None, :]
    scores = jnp.where(causal[None, None], scores, jnp.float32(0.0))
    intra = jnp.einsum("nhts,nshe->nthe", scores, va.astype(jnp.float32), precision=highest)
    heads_out = (inter + intra).reshape(rows, heads, HD)
    scale = lax.rsqrt(jnp.mean(heads_out * heads_out, axis=-1, keepdims=True) + 1e-05)
    normed = (heads_out * scale).reshape(rows, heads * HD)
    attn = (normed * norm_gain[None, :] * jax.nn.sigmoid(gate.astype(jnp.float32))).astype(
        jnp.bfloat16
    )
    return lax.psum_scatter(
        jnp.dot(attn, w_out, preferred_element_type=jnp.float32).astype(jnp.bfloat16),
        "tp",
        scatter_dimension=0,
        tiled=True,
    )


def solution(mesh):
    in_specs = (
        P("seq", "tp"),
        P("seq", "tp"),
        P("seq", "tp"),
        P("seq", "tp"),
        P("tp", None, None),
        P("tp"),
        P("tp", None),
    )
    out_specs = P(("seq", "tp"), None)
    return jax.shard_map(
        per_device, mesh=mesh, in_specs=in_specs, out_specs=out_specs, check_vma=False
    )
```

profile of v0, /device:TPU:2, one launch (start us, length us, event | category | flops | bytes accessed | tf_op | source)
XLA Modules:
  0.0 170.8 jit_solution(4474242960137433406)
XLA Ops:
  6.5 0.0 all-gather.3.cloned.1.call-start
  6.5 1.8 %fusion.8 = bf16[1024,512]{1,0:T(8,128)(2,1)S(1)} fusion(bf16[1024,512]{1,0:T(8,128)(2,1)} %param.8), kind=kLoop, calls=%fused_computation.14 | loop fusion | flops 3145728 | bytes 2097152 | tf_op jit(solution)/shard_map/convert_element_type | solution.py:20
  8.4 0.3 reshape.60
  8.7 1.3 reshape.61
  10.0 0.7 copy.33
  10.7 0.0 copy-start.3
  10.7 2.0 %fusion.28 = (bf16[4,128,128]{2,1,0:T(8,128)(2,1)}, f32[2,4,128,128]{3,2,1,0:T(8,128)}) fusion(bf16[2,512,4,128]{1,3,2,0:T(8,128)(2,1)S(1)} %copy.33, bf16[2,512,4,128]{3,2,1,0:T(4,128)(2,1)S(1)} %reshape.60), kind=kOutput, calls=%fused_computation.40 | convolution fusion | flops 134283264 | bytes 2752512 | tf_op jit(solution)/shard_map/nthd,nthe->nhde/dot_general | solution.py:24
  12.7 0.0 all-gather.3.cloned.1.call-update
  12.7 0.0 reduce-scatter.2.cloned.1.call-start
  12.7 0.0 copy-done.3
  12.7 1.6 fusion.12
  14.3 1.3 reshape.62
  15.7 0.1 iota_compare_fusion
  15.8 1.3 fusion.22
  17.0 6.7 %fusion = f32[2,4,512,128]{2,3,1,0:T(8,128)} fusion(bf16[2,512,4,128]{1,3,2,0:T(8,128)(2,1)S(1)} %copy.33, f32[2,4,512,512]{3,2,1,0:T(8,128)S(1)} %fusion.22, pred[512,512]{1,0:T(8,128)(4,1)S(1)} %iota_compare_fusion), kind=kOutput, calls=%fused_computation.1 | convolution fusion | flops 3223322624 | bytes 11796480 | tf_op jit(solution)/shard_map/nhts,nshe->nthe/dot_general | solution.py:39
  23.7 0.0 copy-start.4
  23.7 0.0 copy-start.1
  23.7 41.7 %all-gather.3.cloned.1.call-done = bf16[64,128,128]{2,1,0:T(8,128)(2,1)} async-done(((bf16[4,128,128]{2,1,0:T(8,128)(2,1)}), bf16[64,128,128]{2,1,0:T(8,128)(2,1)}) %all-gather.3.cloned.1.call-update) | async-done | bytes 2097168 | tf_op jit(solution)/shard_map/all_gather | solution.py:27
  65.4 0.0 copy-start
  65.4 2.2 %fusion.2 = f32[4,128,128]{2,1,0:T(8,128)S(1)} fusion(bf16[16,4,128,128]{3,2,1,0:T(8,128)(2,1)} %bitcast.27, f32[16]{0:T(128)S(1)} %compare_convert_fusion), kind=kLoop, calls=%fused_computation.4 | loop fusion | flops 3080192 | bytes 2359360 | tf_op jit(solution)/shard_map/reduce_sum | solution.py:32
  67.6 0.0 copy-done.4
  67.7 0.0 copy-done.1
  67.7 0.1 fusion.16
  67.9 0.0 copy-done
  67.9 1.3 multiply_reduce_fusion
  69.2 0.2 copy.35
  69.4 1.9 %copy.34 = f32[2,512,4,128]{3,2,1,0:T(4,128)} copy(f32[2,512,4,128]{1,3,2,0:T(8,128)S(1)} %get-tuple-element.8) | data formatting | bytes 4194304 | tf_op jit(solution)/shard_map/add | solution.py:40
  71.3 0.0 copy-start.2
  71.3 0.0 copy-start.5
  71.3 1.2 mul.46
  72.5 0.4 copy-done.2
  72.8 0.0 copy-done.5
  72.8 11.9 %convolution_convert_fusion = bf16[1024,6144]{1,0:T(8,128)(2,1)} fusion(bf16[512,6144]{1,0:T(8,128)(2,1)} %param.13, f32[128,8,4,128]{3,2,1,0:T(4,128)S(1)} %bitcast.28, f32[128,8,4,128]{3,2,1,0:T(4,128)S(1)} %bitcast.29, bf16[1024,512]{1,0:T(8,128)(2,1)} %param.10, f32[512]{0:T(512)S(1)} %copy-done.5), kind=kOutput, calls=%fused_computation | convolution fusion | flops 6452936704 | bytes 24119296 | tf_op jit(solution)/shard_map/dot_general | solution.py:47
  84.7 0.0 reduce-scatter.2.cloned.1.call-update
  84.8 79.2 %reduce-scatter.2.cloned.1.call-done = bf16[64,6144]{1,0:T(8,128)(2,1)} async-done(((bf16[1024,6144]{1,0:T(8,128)(2,1)}), bf16[64,6144]{1,0:T(8,128)(2,1)}) %reduce-scatter.2.cloned.1.call-update) | async-done | bytes 786448 | tf_op jit(solution)/shard_map/reduce_scatter | solution.py:46
  (3 shorter events, 0.1 us)
Async XLA Ops:
  6.5 58.8 %all-gather.3.cloned.1.call-start = ((), (), s32[]{:S(2)}) async-start(), calls=%async_computation.2 | async-start | bytes 2228224 | tf_op jit(solution)/shard_map/all_gather | solution.py:27
  10.7 2.1 %copy-start.3 = (bf16[1024,512]{1,0:T(8,128)(2,1)S(1)}, bf16[1024,512]{1,0:T(8,128)(2,1)}, u32[]{:S(2)}) copy-start(bf16[1024,512]{1,0:T(8,128)(2,1)} %param.7) | copy-start | bytes 3145732
  12.7 151.3 %reduce-scatter.2.cloned.1.call-start = ((), (), s32[]{:S(2)}) async-start(), calls=%async_computation.1 | async-start | bytes 13369344 | tf_op jit(solution)/shard_map/reduce_scatter | solution.py:46
  23.7 43.9 %copy-start.4 = (f32[4,128,128]{2,1,0:T(8,128)S(1)}, f32[4,128,128]{2,1,0:T(8,128)}, u32[]{:S(2)}) copy-start(f32[4,128,128]{2,1,0:T(8,128)} %param.11) | copy-start | bytes 786436
  23.7 44.0 %copy-start.1 = (f32[2,4,128,128]{3,2,1,0:T(8,128)S(1)}, f32[2,4,128,128]{3,2,1,0:T(8,128)}, u32[]{:S(2)}) copy-start(f32[2,4,128,128]{3,2,1,0:T(8,128)} %get-tuple-element.6) | copy-start | bytes 1572868
  65.4 2.5 %copy-start = (f32[2,4,512,128]{2,3,1,0:T(8,128)S(1)}, f32[2,4,512,128]{2,3,1,0:T(8,128)}, u32[]{:S(2)}) copy-start(f32[2,4,512,128]{2,3,1,0:T(8,128)} %fusion) | copy-start | bytes 6291460
  71.3 1.6 copy-start.2
  71.3 1.6 copy-start.5
Sparse Core Ops, SparseCore 0:
  12.8 52.5 all-gather.2
  84.9 79.0 reduce-scatter.1
where the time goes:
time: 171 us
  waiting for transfers between devices  121 us (71%)
  matrix products  23 us (13%)
  between operations  13.6 us (8%)
  local copies, waits for them, and re-layouts  7.34 us (4%)
  other arithmetic  5.92 us (3%)
    reduce_scatter x1, waiting for transfers between devices, per_device(): lax.psum_scatter(jnp.dot(attn, w_out, preferred_element_type=jnp.float32)...  79.2 us
    all_gather x1, waiting for transfers between devices, per_device(): lax.all_gather(own_total[None].astype(jnp.bfloat16), 'seq', axis=0, tiled...  41.7 us
    dot_general x1, matrix products, per_device(): jnp.dot(attn, w_out, preferred_element_type=jnp.float32)  11.9 us
    dot_general x1, matrix products, per_device(): jnp.einsum('nhts,nshe->nthe', scores, va.astype(jnp.float32), precision=h...  6.66 us
  transfers between devices with their start and end apart: 2, of which 2 were waited for; matrix products, arithmetic and copies ran while one was open for 6% of the time, Pallas kernels for 0%

commit v1 on v0

--- a/solution.py
+++ b/solution.py
@@ -1,9 +1,20 @@
+import functools
 import jax
 import jax.numpy as jnp
 from jax import lax
 from jax.sharding import PartitionSpec as P
 
 HD = 128
+
+
+def lead_floor_on_mesh(xx, in_dim):
+    return jnp.concatenate(
+        lax.all_to_all(jnp.stack(lax.axis_size("seq") * [xx]), "seq", concat_axis=0, split_axis=0),
+        axis=in_dim,
+    )
+
+
+shape_state = functools.partial(lead_floor_on_mesh, in_dim=0)
 
 
 def per_device(query, key_in, value, gate, kv_start, norm_gain, w_out):
@@ -24,9 +35,7 @@
     block_states = jnp.einsum("nthd,nthe->nhde", ka, va, preferred_element_type=jnp.float32)
     own_total = jnp.sum(block_states, axis=0)
     local_before = jnp.cumsum(block_states, axis=0) - block_states
-    gathered = lax.all_gather(
-        own_total[None].astype(jnp.bfloat16), "seq", axis=0, tiled=True
-    ).astype(jnp.float32)
+    gathered = shape_state(own_total[None].astype(jnp.bfloat16)).astype(jnp.float32)
     position = lax.axis_index("seq")
     below = (jnp.arange(gathered.shape[0]) < position).astype(jnp.float32)
     prior = jnp.sum(gathered * below[:, None, None, None], axis=0)

time: 171 us -> 157 us (0.918)
  waiting for transfers between devices: 121 us -> 97.9 us
  starting transfers between devices: 0.04 us -> 7.83 us
  local copies, waits for them, and re-layouts: 7.34 us -> 9.14 us
    all_gather x1 -> x0, waiting for transfers between devices: 41.7 us -> none  [per_device(): lax.all_gather(own_total[None].astype(jnp.bfloat16), 'seq', axis=0, tiled...]
    all_to_all x0 -> x1, waiting for transfers between devices: none -> 16 us  [lead_floor_on_mesh(): lax.all_to_all(jnp.stack(lax.axis_size('seq') * [xx]), 'seq', concat_axis...]
    all_to_all x0 -> x1, starting transfers between devices: none -> 7.61 us  [lead_floor_on_mesh(): lax.all_to_all(jnp.stack(lax.axis_size('seq') * [xx]), 'seq', concat_axis...]
    reduce_scatter x1, waiting for transfers between devices: 79.2 us -> 81.8 us  [per_device(): lax.psum_scatter(jnp.dot(attn, w_out, preferred_element_type=jnp.float32)...]
    another operation x0 -> x1, local copies, waits for them, and re-layouts: none -> 1.8 us  [lead_floor_on_mesh(): jnp.stack(lax.axis_size('seq') * [xx])]
  transfers between devices with their start and end apart: 2 -> 2, of which waited for: 2 -> 2; matrix products, arithmetic and copies ran while one was open for 6% -> 7% of each run, Pallas kernels for 0% -> 0%
where the time goes in v1:
time: 157 us
  waiting for transfers between devices  97.9 us (62%)
  matrix products  22.4 us (14%)
  between operations  13.6 us (9%)
  local copies, waits for them, and re-layouts  9.14 us (6%)
  starting transfers between devices  7.83 us (5%)
  other arithmetic  5.91 us (4%)
    reduce_scatter x1, waiting for transfers between devices, per_device(): lax.psum_scatter(jnp.dot(attn, w_out, preferred_element_type=jnp.float32)...  81.8 us
    all_to_all x1, waiting for transfers between devices, lead_floor_on_mesh(): lax.all_to_all(jnp.stack(lax.axis_size('seq') * [xx]), 'seq', concat_axis...  16 us
    dot_general x1, matrix products, per_device(): jnp.dot(attn, w_out, preferred_element_type=jnp.float32)  11.9 us
    all_to_all x1, starting transfers between devices, lead_floor_on_mesh(): lax.all_to_all(jnp.stack(lax.axis_size('seq') * [xx]), 'seq', concat_axis...  7.61 us
    dot_general x1, matrix products, per_device(): jnp.einsum('nhts,nshe->nthe', scores, va.astype(jnp.float32), precision=h...  6.7 us
  transfers between devices with their start and end apart: 2, of which 2 were waited for; matrix products, arithmetic and copies ran while one was open for 7% of the time, Pallas kernels for 0%

profile of v1, /device:TPU:2, one launch (start us, length us, event | category | flops | bytes accessed | tf_op | source)
XLA Modules:
  0.0 156.7 jit_solution(2376800612872693562)
XLA Ops:
  6.5 1.8 %fusion.8 = bf16[1024,512]{1,0:T(8,128)(2,1)S(1)} fusion(bf16[1024,512]{1,0:T(8,128)(2,1)} %param.8), kind=kLoop, calls=%fused_computation.14 | loop fusion | flops 3145728 | bytes 2097152 | tf_op jit(solution)/shard_map/convert_element_type | solution.py:31
  8.4 0.3 reshape.62
  8.7 1.3 reshape.63
  10.0 0.7 copy.51
  10.7 1.3 fusion.28
  12.0 1.8 %stack.2 = bf16[16,1,4,128,128]{4,3,2,1,0:T(8,128)(2,1)} broadcast(bf16[4,128,128]{2,1,0:T(8,128)(2,1)S(1)} %get-tuple-element.5), dimensions={2,3,4} | broadcast | bytes 2228224 | tf_op jit(solution)/shard_map/stack | solution.py:12
  13.8 0.0 copy-start.3
  13.8 7.6 %all-to-all-start = ((bf16[16,1,4,128,128]{4,3,2,1,0:T(8,128)(2,1)}), bf16[16,1,4,128,128]{4,3,2,1,0:T(8,128)(2,1)}, u32[]{:S(2)}, u32[]{:S(2)}) async-start(bf16[16,1,4,128,128]{4,3,2,1,0:T(8,128)(2,1)} %stack.2), calls=%async_computation | async-start | bytes 4194304 | tf_op jit(solution)/shard_map/all_to_all | solution.py:12
  21.4 0.2 reduce-scatter.2.cloned.1.call-start
  21.6 0.0 copy-done.3
  21.6 1.6 %fusion.12 = bf16[1024,512]{1,0:T(8,128)(2,1)} fusion(bf16[1024,512]{1,0:T(8,128)(2,1)S(1)} %copy-done.3), kind=kLoop, calls=%fused_computation.18 | loop fusion | flops 3145728 | bytes 2097152 | tf_op jit(solution)/shard_map/convert_element_type | solution.py:27
  23.2 1.3 reshape.64
  24.6 0.1 iota_compare_fusion
  24.7 1.3 fusion.22
  25.9 6.7 %fusion = f32[2,4,512,128]{2,3,1,0:T(8,128)} fusion(bf16[2,512,4,128]{1,3,2,0:T(8,128)(2,1)S(1)} %copy.51, f32[2,4,512,512]{3,2,1,0:T(8,128)S(1)} %fusion.22, pred[512,512]{1,0:T(8,128)(4,1)S(1)} %iota_compare_fusion), kind=kOutput, calls=%fused_computation.1 | convolution fusion | flops 3223322624 | bytes 11796480 | tf_op jit(solution)/shard_map/nhts,nshe->nthe/dot_general | solution.py:48
  32.6 0.0 copy-start.4
  32.6 0.0 copy-start.1
  32.6 16.0 %all-to-all-done = bf16[16,1,4,128,128]{4,3,2,1,0:T(8,128)(2,1)} async-done(((bf16[16,1,4,128,128]{4,3,2,1,0:T(8,128)(2,1)}), bf16[16,1,4,128,128]{4,3,2,1,0:T(8,128)(2,1)}, u32[]{:S(2)}, u32[]{:S(2)}) %all-to-all-start) | async-done | bytes 2097184 | tf_op jit(solution)/shard_map/all_to_all | solution.py:12
  48.7 0.0 copy-start
  48.7 2.2 %fusion.2 = f32[4,128,128]{2,1,0:T(8,128)S(1)} fusion(bf16[16,1,4,128,128]{4,3,2,1,0:T(8,128)(2,1)} %all-to-all-done, f32[16]{0:T(128)S(1)} %compare_convert_fusion), kind=kLoop, calls=%fused_computation.4 | loop fusion | flops 3080192 | bytes 2359360 | tf_op jit(solution)/shard_map/reduce_sum | solution.py:41
  50.9 0.0 copy-done.4
  51.0 0.0 copy-done.1
  51.0 0.1 fusion.16
  51.1 0.0 copy-done
  51.1 1.3 multiply_reduce_fusion
  52.4 0.2 copy.53
  52.7 1.9 %copy.52 = f32[2,512,4,128]{3,2,1,0:T(4,128)} copy(f32[2,512,4,128]{1,3,2,0:T(8,128)S(1)} %get-tuple-element.8) | data formatting | bytes 4194304 | tf_op jit(solution)/shard_map/add | solution.py:49
  54.5 0.0 copy-start.2
  54.5 0.0 copy-start.5
  54.5 1.2 mul.46
  55.8 0.4 copy-done.2
  56.1 0.0 copy-done.5
  56.1 11.9 %convolution_convert_fusion = bf16[1024,6144]{1,0:T(8,128)(2,1)} fusion(bf16[512,6144]{1,0:T(8,128)(2,1)} %param.13, f32[128,8,4,128]{3,2,1,0:T(4,128)S(1)} %bitcast.28, f32[128,8,4,128]{3,2,1,0:T(4,128)S(1)} %bitcast.29, bf16[1024,512]{1,0:T(8,128)(2,1)} %param.10, f32[512]{0:T(512)S(1)} %copy-done.5), kind=kOutput, calls=%fused_computation | convolution fusion | flops 6452936704 | bytes 24119296 | tf_op jit(solution)/shard_map/dot_general | solution.py:56
  68.0 0.0 reduce-scatter.2.cloned.1.call-update
  68.1 81.8 %reduce-scatter.2.cloned.1.call-done = bf16[64,6144]{1,0:T(8,128)(2,1)} async-done(((bf16[1024,6144]{1,0:T(8,128)(2,1)}), bf16[64,6144]{1,0:T(8,128)(2,1)}) %reduce-scatter.2.cloned.1.call-update) | async-done | bytes 786448 | tf_op jit(solution)/shard_map/reduce_scatter | solution.py:55
  (3 shorter events, 0.1 us)
Async XLA Ops:
  13.8 7.8 %copy-start.3 = (bf16[1024,512]{1,0:T(8,128)(2,1)S(1)}, bf16[1024,512]{1,0:T(8,128)(2,1)}, u32[]{:S(2)}) copy-start(bf16[1024,512]{1,0:T(8,128)(2,1)} %param.7) | copy-start | bytes 3145732
  13.8 34.9 %all-to-all-start = ((bf16[16,1,4,128,128]{4,3,2,1,0:T(8,128)(2,1)}), bf16[16,1,4,128,128]{4,3,2,1,0:T(8,128)(2,1)}, u32[]{:S(2)}, u32[]{:S(2)}) async-start(bf16[16,1,4,128,128]{4,3,2,1,0:T(8,128)(2,1)} %stack.2), calls=%async_computation | async-start | bytes 4194304 | tf_op jit(solution)/shard_map/all_to_all | solution.py:12
  21.4 128.5 %reduce-scatter.2.cloned.1.call-start = ((), (), s32[]{:S(2)}) async-start(), calls=%async_computation.2 | async-start | bytes 13369344 | tf_op jit(solution)/shard_map/reduce_scatter | solution.py:55
  32.6 18.3 %copy-start.4 = (f32[4,128,128]{2,1,0:T(8,128)S(1)}, f32[4,128,128]{2,1,0:T(8,128)}, u32[]{:S(2)}) copy-start(f32[4,128,128]{2,1,0:T(8,128)} %param.11) | copy-start | bytes 786436
  32.6 18.3 %copy-start.1 = (f32[2,4,128,128]{3,2,1,0:T(8,128)S(1)}, f32[2,4,128,128]{3,2,1,0:T(8,128)}, u32[]{:S(2)}) copy-start(f32[2,4,128,128]{3,2,1,0:T(8,128)} %get-tuple-element.6) | copy-start | bytes 1572868
  48.7 2.5 %copy-start = (f32[2,4,512,128]{2,3,1,0:T(8,128)S(1)}, f32[2,4,512,128]{2,3,1,0:T(8,128)}, u32[]{:S(2)}) copy-start(f32[2,4,512,128]{2,3,1,0:T(8,128)} %fusion) | copy-start | bytes 6291460
  54.5 1.6 %copy-start.2 = (f32[2,512,4,128]{3,2,1,0:T(4,128)S(1)}, f32[2,512,4,128]{3,2,1,0:T(4,128)}, u32[]{:S(2)}) copy-start(f32[2,512,4,128]{3,2,1,0:T(4,128)} %copy.52) | copy-start | bytes 6291460
  54.5 1.6 %copy-start.5 = (f32[512]{0:T(512)S(1)}, f32[512]{0:T(512)}, u32[]{:S(2)}) copy-start(f32[512]{0:T(512)} %param.12) | copy-start | bytes 6148
Sparse Core Ops, SparseCore 0:
  68.2 81.6 reduce-scatter.1
